TPU v7x, 512 devices: a whole 4x4x16 slice. The times are simulated.
512 devices in a mesh: dp: 128 (over x, z, core), bin: 4 (over y).
Axes of the slice: x: 4, y: 4, z: 16, core: 2. Of those that a mesh axis runs over, the one named last changes fastest.
Arguments:
- features: bfloat16 [65536, 2, 2048], P(('dp', 'bin')), may hold values from -90 to 90
- head_weight: bfloat16 [2048, 1024], P('bin'), may hold values from -9 to 9
- bin_of_row: int32 [65536, 1], P(('dp', 'bin')), may hold values from 0 to 191; in each aligned block of 128 rows (0 to 127, 128 to 255, ...) at most 2 rows name the same one
- bin_owner: int32 [192], replicated, may hold values from 0 to 127, never falling along the last dimension, each value on 1 to 2 neighbouring positions
- bin_link: int32 [192], replicated, may hold values 0 or 1
Outputs:
- grad_rows: bfloat16 [65536, 2, 1024], P(('dp', 'bin'))
- grad_weight: float32 [2048, 1024], P(('bin', 'dp'))
Inputs may be any that keep to these rules, and one draw needn't show every extreme that they name: `bin_of_row`: in the rows of one device no bin appears more than 2 times. `bin_owner`: never falls; every owner holds 1 to 2 consecutive bins.
All inputs are finite; a program needn't handle non-finite values.
Results may differ from a plain program's by a relative error of at most 0.012.
Values may be sent and summed in bfloat16 or wider, within the bound.
No kernel may reach another device: no remote copies, remote signals or barrier semaphores. Data moves between devices by JAX's collectives and lax.ppermute only.
A program may use at most 64 MiB of HBM per device.

v0:
```python
import jax
import jax.numpy as jnp
from jax import lax
from jax.sharding import Mesh
from jax.sharding import PartitionSpec as P

MOSTB = 2
SOFTMAX_TEMP_SCALE = 0.1
DP_PARTS = (("dx", 4), ("dz", 16), ("dc", 2))
DP = tuple((name for name, _ in DP_PARTS))
EMPTY_MARK = 4.0


def allowed_mask(valid, first, bin_link, group_slots, per_bin):
    per_owner = per_bin * MOSTB
    position = jnp.arange(group_slots, dtype=jnp.int32)
    local_bin = position % per_owner // per_bin
    padded = jnp.concatenate([bin_link, jnp.zeros((MOSTB,), jnp.int32)])
    nearby = lax.dynamic_slice(padded, (first,), (MOSTB,))
    lower = jnp.minimum(local_bin[:, None], local_bin[None, :])
    linked = jnp.zeros((group_slots, group_slots), jnp.int32)
    for height in range(MOSTB):
        linked = linked + jnp.where(lower == height, nearby[height], 0)
    spacing = jnp.abs(local_bin[:, None] - local_bin[None, :])
    paired = valid[:, None] & valid[None, :]
    allowed = paired & ((spacing == 0) | (spacing == 1) & (linked == 1))
    allowed = allowed | (position[:, None] == position[None, :])
    return allowed.astype(jnp.float32)


def contrast(query_rows, key_matrix, allowed, valid):
    similarity_scores = (
        lax.dot_general(
            query_rows, key_matrix, (((1,), (1,)), ((), ())), preferred_element_type=jnp.float32
        )
        / SOFTMAX_TEMP_SCALE
    )
    weights = allowed * jnp.exp(similarity_scores)
    shares = weights / jnp.sum(weights, axis=1, keepdims=True)
    position = jnp.arange(query_rows.shape[0], dtype=jnp.int32)
    diagonal = (position[:, None] == position[None, :]).astype(jnp.float32)
    logit_gradient = ((shares - diagonal) * valid[:, None]).astype(jnp.bfloat16)
    query_gradient = (
        jnp.dot(logit_gradient, key_matrix, preferred_element_type=jnp.float32) / SOFTMAX_TEMP_SCALE
    ).astype(jnp.bfloat16)
    key_gradient_rows = (
        lax.dot_general(
            logit_gradient, query_rows, (((0,), (0,)), ((), ())), preferred_element_type=jnp.float32
        )
        / SOFTMAX_TEMP_SCALE
    ).astype(jnp.bfloat16)
    return jnp.stack([query_gradient, key_gradient_rows], axis=1)


def dp_index():
    index = 0
    for name, size in DP_PARTS:
        index = index * size + lax.axis_index(name)
    return index


def local(features, head_weight, bin_of_row, bin_owner, bin_link):
    rows_dev, views, feat_dim = features.shape
    part_rows, emb_dim = head_weight.shape
    sources = 1
    for _, size in DP_PARTS:
        sources *= size
    bins_n = lax.axis_size("bin")
    bin_count = bin_owner.shape[0]
    per_bin = max(2, 2 * rows_dev // bin_count)
    per_owner = per_bin * MOSTB
    group_slots = sources * per_owner
    flat = features.reshape(rows_dev * views, feat_dim)
    folded = jnp.dot(
        flat,
        lax.all_gather(head_weight, "bin", axis=0, tiled=True),
        preferred_element_type=jnp.float32,
    )
    embedded = folded.reshape(rows_dev, views, emb_dim)
    scale = lax.rsqrt(jnp.sum(embedded * embedded, axis=2, keepdims=True) + 1e-06)
    unit = embedded * scale
    sent = unit.astype(jnp.bfloat16)
    row_bins = bin_of_row[:, 0]
    lookup = row_bins[:, None] == jnp.arange(bin_count, dtype=jnp.int32)[None, :]
    owner = jnp.sum(jnp.where(lookup, bin_owner[None, :], 0), axis=1)
    first_by_bin = jnp.sum((bin_owner[None, :] < bin_owner[:, None]).astype(jnp.int32), axis=1)
    local_bin = row_bins - jnp.sum(jnp.where(lookup, first_by_bin[None, :], 0), axis=1)
    order = jnp.arange(rows_dev, dtype=jnp.int32)
    earlier = (row_bins[:, None] == row_bins[None, :]) & (order[None, :] < order[:, None])
    seat = jnp.sum(earlier.astype(jnp.int32), axis=1)
    target = owner * per_owner + local_bin * per_bin + seat
    empty = jnp.zeros((group_slots, views, emb_dim), jnp.bfloat16).at[:, 0, 0].set(EMPTY_MARK)
    outbox = empty.at[target].set(sent)
    inbox = lax.all_to_all(
        outbox.reshape(sources, per_owner, views, emb_dim),
        DP,
        split_axis=0,
        concat_axis=0,
        tiled=True,
    )
    inbox = inbox.reshape(group_slots, views, emb_dim)
    valid = inbox[:, 0, 0] < 2.0
    inbox = jnp.where(valid[:, None, None], inbox, jnp.zeros_like(inbox))
    first = jnp.sum((bin_owner < dp_index()).astype(jnp.int32))
    allowed = allowed_mask(valid, first, bin_link, group_slots, per_bin)
    grads = contrast(inbox[:, 0], inbox[:, 1], allowed, valid.astype(jnp.float32))
    returned = lax.all_to_all(
        grads.reshape(sources, per_owner, views, emb_dim),
        DP,
        split_axis=0,
        concat_axis=0,
        tiled=True,
    )
    row_grads = returned.reshape(group_slots, views, emb_dim)[target].astype(jnp.float32)
    grad_rows = (
        scale * (row_grads - unit * jnp.sum(unit * row_grads, axis=2, keepdims=True))
    ).astype(jnp.bfloat16)
    columns = lax.all_to_all(
        features.reshape(rows_dev, views, bins_n, part_rows),
        "bin",
        split_axis=2,
        concat_axis=0,
        tiled=True,
    )
    outgrad = lax.all_gather(grad_rows, "bin", axis=0, tiled=True)
    count = columns.shape[0]
    sizes = [size for _, size in DP_PARTS]
    columns = columns.reshape(count * views, *sizes, part_rows // sources)
    columns = jnp.transpose(columns, (0, 3, 2, 1, 4)).reshape(count * views, part_rows)
    local_grad = lax.dot_general(
        columns,
        outgrad.reshape(count * views, emb_dim),
        (((0,), (0,)), ((), ())),
        preferred_element_type=jnp.float32,
    )
    for name in ("dc", "dz", "dx"):
        local_grad = lax.psum_scatter(local_grad, name, scatter_dimension=0, tiled=True)
    grad_weight = local_grad / rows_dev
    return (grad_rows, grad_weight)


def solution(mesh):
    sizes = [size for _, size in DP_PARTS]
    devices = mesh.devices.reshape(*sizes, mesh.devices.shape[1])
    parted = Mesh(devices, (*DP, "bin"))
    return jax.shard_map(
        local,
        mesh=parted,
        in_specs=(P((*DP, "bin"), None, None), P("bin", None), P((*DP, "bin"), None), P(), P()),
        out_specs=(P((*DP, "bin"), None, None), P(("bin", *DP), None)),
        check_vma=False,
    )
```

profile of v0, /device:TPU:8, one launch (start us, length us, event | category | flops | bytes accessed | tf_op | source)
XLA Modules:
  0.0 661.2 jit_solution(16799873341460603890)
XLA Ops:
  7.9 0.9 convert_reduce_fusion.1
  8.8 0.9 convert_reduce_fusion
  9.8 0.8 select_reduce_fusion.1
  11.2 58.6 %all-gather.3.cloned.1.call-done = bf16[2048,1024]{1,0:T(8,128)(2,1)} async-done(((bf16[512,1024]{1,0:T(8,128)(2,1)}), bf16[2048,1024]{1,0:T(8,128)(2,1)}) %all-gather.3.cloned.1.call-update) | async-done | bytes 4194320 | tf_op jit(solution)/shard_map/all_gather | solution.py:76
  69.8 3.9 multiply_reduce_fusion
  73.9 0.8 copy-done.3
  75.3 1.1 scatter.12
  76.4 4.3 scatter_fusion
  80.7 1.3 copy-done
  82.0 17.0 %all-to-all-start = ((bf16[128,4,2,1024]{3,2,1,0:T(2,128)(2,1)}), bf16[128,4,2,1024]{3,2,1,0:T(2,128)(2,1)S(1)}, u32[]{:S(2)}, u32[]{:S(2)}) async-start(bf16[128,4,2,1024]{3,2,1,0:T(2,128)(2,1)} %bitcast.64), calls=%async_computation | async-start | bytes 4194304 | tf_op jit(solution)/shard_map/all_to_all | solution.py:94
  102.3 95.6 %all-to-all-done = bf16[128,4,2,1024]{3,2,1,0:T(2,128)(2,1)S(1)} async-done(((bf16[128,4,2,1024]{3,2,1,0:T(2,128)(2,1)}), bf16[128,4,2,1024]{3,2,1,0:T(2,128)(2,1)S(1)}, u32[]{:S(2)}, u32[]{:S(2)}) %all-to-all-start) | async-done | bytes 2097184 | tf_op jit(solution)/shard_map/all_to_all | solution.py:94
  199.0 2.7 fusion.32
  204.0 2.7 pad_maximum_fusion
  206.8 9.2 %all-to-all-start.1 = ((bf16[128,4,2,1024]{3,1,2,0:T(4,128)(2,1)}), bf16[128,4,2,1024]{3,1,2,0:T(4,128)(2,1)S(1)}, u32[]{:S(2)}, u32[]{:S(2)}) async-start(bf16[128,4,2,1024]{3,1,2,0:T(4,128)(2,1)} %pad_maximum_fusion), calls=%async_computation.1 | async-start | bytes 4194304 | tf_op jit(solution)/shard_map/all_to_all | solution.py:107
  216.0 98.8 %all-to-all-done.1 = bf16[128,4,2,1024]{3,1,2,0:T(4,128)(2,1)S(1)} async-done(((bf16[128,4,2,1024]{3,1,2,0:T(4,128)(2,1)}), bf16[128,4,2,1024]{3,1,2,0:T(4,128)(2,1)S(1)}, u32[]{:S(2)}, u32[]{:S(2)}) %all-to-all-start.1) | async-done | bytes 2097184 | tf_op jit(solution)/shard_map/all_to_all | solution.py:107
  314.8 3.8 copy.37
  318.6 3.3 gather_fusion
  321.9 2.1 fusion.9
  324.8 23.8 %all_to_all.25 = bf16[128,2,4,512]{3,1,0,2:T(2,128)(2,1)S(1)} all-to-all(bf16[128,2,4,512]{3,1,0,2:T(2,128)(2,1)S(1)} %bitcast.66), channel_id=1, replica_groups=mesh['dx'=4,'dz'=16,'dc'=2,'bin'=4] {'bin'}, dimensions={2} | all-to-all | bytes 2097152 | tf_op jit(solution)/shard_map/all_to_all | solution.py:118
  348.6 73.1 %reshape.155 = bf16[1024,4,16,2,4]{4,3,2,1,0:T(2,128)(2,1)} reshape(bf16[4,128,2,1,512]{4,2,1,0,3:T(2,128)(2,1)S(1)} %bitcast.65) | data formatting | bytes 2097152 | tf_op jit(solution)/shard_map/reshape | solution.py:128
  421.7 76.1 %copy.41 = bf16[1024,2,16,4,4]{0,4,3,2,1:T(4,128)(2,1)S(1)} copy(bf16[1024,2,16,4,4]{4,1,2,3,0:T(2,128)(2,1)} %bitcast.61) | data formatting | bytes 2097152 | tf_op jit(solution)/shard_map/transpose | solution.py:129
  498.1 3.7 copy.39
  501.9 2.2 reshape.153
  504.1 4.2 convolution_bitcast_fusion
  508.5 11.2 %reduce-scatter.6.cloned.1.call-done = f32[256,1024]{0,1:T(8,128)} async-done(((f32[512,1024]{0,1:T(8,128)}), f32[256,1024]{0,1:T(8,128)}) %reduce-scatter.6.cloned.1.call-update) | async-done | bytes 1048592 | tf_op jit(solution)/shard_map/reduce_scatter | solution.py:137
  519.6 2.5 copy.45
  522.3 72.0 %reduce-scatter.8.cloned.1.call-done = f32[16,1024]{1,0:T(8,128)} async-done(((f32[256,1024]{1,0:T(8,128)}), f32[16,1024]{1,0:T(8,128)}) %reduce-scatter.8.cloned.1.call-update) | async-done | bytes 65552
  594.3 1.8 copy.46
  596.2 1.3 dynamic-slice.6
  598.1 1.3 copy.42
  599.4 53.2 %all-reduce.4.cloned.1.call-done = f32[16,1024]{0,1:T(8,128)} async-done(((f32[16,1024]{0,1:T(8,128)}), f32[16,1024]{0,1:T(8,128)}) %all-reduce.4.cloned.1.call-update) | async-done | bytes 65552
  652.7 1.2 dynamic-slice_multiply_fusion
  (45 shorter events, 8.9 us)
Async XLA Ops:
  7.2 62.7 %all-gather.3.cloned.1.call-start = ((), (), s32[]{:S(2)}) async-start(), calls=%async_computation.5 | async-start | bytes 5242880 | tf_op jit(solution)/shard_map/all_gather | solution.py:76
  73.7 1.0 copy-start.3
  73.7 1.5 copy-start.6
  80.7 1.4 copy-start
  82.0 17.0 %copy-start.5 = (s32[192]{0:T(256)S(1)}, s32[192]{0:T(256)}, u32[]{:S(2)}) copy-start(s32[192]{0:T(256)} %param.10) | copy-start | bytes 2308
  82.0 19.6 %copy-start.7 = (s32[192]{0:T(256)S(1)}, s32[192]{0:T(256)}, u32[]{:S(2)}) copy-start(s32[192]{0:T(256)} %param.11) | copy-start | bytes 2308
  82.0 115.8 %all-to-all-start = ((bf16[128,4,2,1024]{3,2,1,0:T(2,128)(2,1)}), bf16[128,4,2,1024]{3,2,1,0:T(2,128)(2,1)S(1)}, u32[]{:S(2)}, u32[]{:S(2)}) async-start(bf16[128,4,2,1024]{3,2,1,0:T(2,128)(2,1)} %bitcast.64), calls=%async_computation | async-start | bytes 4194304 | tf_op jit(solution)/shard_map/all_to_all | solution.py:94
  206.8 108.0 %all-to-all-start.1 = ((bf16[128,4,2,1024]{3,1,2,0:T(4,128)(2,1)}), bf16[128,4,2,1024]{3,1,2,0:T(4,128)(2,1)S(1)}, u32[]{:S(2)}, u32[]{:S(2)}) async-start(bf16[128,4,2,1024]{3,1,2,0:T(4,128)(2,1)} %pad_maximum_fusion), calls=%async_computation.1 | async-start | bytes 4194304 | tf_op jit(solution)/shard_map/all_to_all | solution.py:107
  216.0 282.2 %all-gather.5.cloned.1.call-start = ((), (), s32[]{:S(2)}) async-start(), calls=%async_computation.6 | async-start | bytes 2621440 | tf_op jit(solution)/shard_map/all_gather | solution.py:125
  216.0 105.8 %copy-start.4 = (f32[128,2,1024]{2,0,1:T(8,128)S(1)}, f32[128,2,1024]{2,0,1:T(8,128)}, u32[]{:S(2)}) copy-start(f32[128,2,1024]{2,0,1:T(8,128)} %copy-done.3) | copy-start | bytes 3145732
  318.6 5.5 copy-start.2
  324.0 195.6 %reduce-scatter.6.cloned.1.call-start = ((), (), s32[]{:S(2)}) async-start(), calls=%async_computation.7 | async-start | bytes 3145728 | tf_op jit(solution)/shard_map/reduce_scatter | solution.py:137
  508.4 89.7 %copy-start.1 = (bf16[128,2,1024]{2,0,1:T(8,128)(2,1)S(1)}, bf16[128,2,1024]{2,0,1:T(8,128)(2,1)}, u32[]{:S(2)}) copy-start(bf16[128,2,1024]{2,0,1:T(8,128)(2,1)} %fusion.9) | copy-start | bytes 1572868
  508.4 85.9 %reduce-scatter.8.cloned.1.call-start = ((), (), s32[]{:S(2)}) async-start(), calls=%async_computation.8 | async-start | bytes 1114112
  522.2 130.5 %all-reduce.4.cloned.1.call-start = ((), (), s32[]{:S(2)}) async-start(), calls=%async_computation.9 | async-start | bytes 1048576
Sparse Core Ops, SparseCore 0:
  10.1 59.6 all-gather.2
  324.1 35.2 all-gather.4
  508.5 11.0 reduce-scatter.5
  522.5 71.7 reduce-scatter.7
  596.5 56.1 all-reduce.3
where the time goes:
time: 663 us; the launch traced here: 661 us
  waiting for transfers between devices  390 us (59%)
  local copies, waits for them, and re-layouts  181 us (27%)
  starting transfers between devices  26.4 us (4%)
  blocking collectives  23.8 us (4%)
  between operations  16.6 us (3%)
  matrix products  12.3 us (2%)
  other arithmetic  10.7 us (2%)
    unnamed x7, waiting for transfers between devices  126 us
    all_to_all x1, waiting for transfers between devices, local(): lax.all_to_all(grads.reshape(sources, per_owner, views, emb_dim), DP, spl...  98.8 us
    all_to_all x1, waiting for transfers between devices, local(): lax.all_to_all(outbox.reshape(sources, per_owner, views, emb_dim), DP, sp...  95.6 us
    transpose x1, local copies, waits for them, and re-layouts, local(): jnp.transpose(columns, (0, 3, 2, 1, 4)).reshape(count * views, part_rows)  76.1 us
    reshape x1, local copies, waits for them, and re-layouts, local(): columns = columns.reshape(count * views, *sizes, part_rows // sources)  73.1 us
    all_gather x1, waiting for transfers between devices, local(): lax.all_gather(head_weight, 'bin', axis=0, tiled=True)  58.6 us
    all_to_all x1, blocking collectives, local(): lax.all_to_all(features.reshape(rows_dev, views, bins_n, part_rows), 'bin...  23.8 us
    all_to_all x1, starting transfers between devices, local(): lax.all_to_all(outbox.reshape(sources, per_owner, views, emb_dim), DP, sp...  17 us
  transfers between devices with their start and end apart: 7, of which 6 were waited for; matrix products, arithmetic and copies ran while one was open for 24% of the time, Pallas kernels for 0%

commit v1 on v0

--- a/solution.py
+++ b/solution.py
@@ -71,11 +71,13 @@
     per_owner = per_bin * MOSTB
     group_slots = sources * per_owner
     flat = features.reshape(rows_dev * views, feat_dim)
-    folded = jnp.dot(
-        flat,
-        lax.all_gather(head_weight, "bin", axis=0, tiled=True),
-        preferred_element_type=jnp.float32,
-    )
+
+    def try_all_shards(mine_x):
+        piece_next = jnp.stack([mine_x for _ in range(jax.lax.axis_size("bin"))], axis=0)
+        base_arr = jax.lax.all_to_all(piece_next, "bin", 0, 0)
+        return jnp.concatenate(base_arr, axis=0)
+
+    folded = jnp.dot(flat, try_all_shards(head_weight), preferred_element_type=jnp.float32)
     embedded = folded.reshape(rows_dev, views, emb_dim)
     scale = lax.rsqrt(jnp.sum(embedded * embedded, axis=2, keepdims=True) + 1e-06)
     unit = embedded * scale

time: 663 us -> 660 us (level)
  waiting for transfers between devices: 390 us -> 373 us
  starting transfers between devices: 26.4 us -> 40.1 us
    all_gather x1 -> x0, waiting for transfers between devices: 58.6 us -> none  [local(): lax.all_gather(head_weight, 'bin', axis=0, tiled=True)]
    all_to_all x0 -> x1, waiting for transfers between devices: none -> 41.9 us  [try_all_shards(): base_arr = jax.lax.all_to_all(piece_next, 'bin', 0, 0)]
    all_to_all x0 -> x1, starting transfers between devices: none -> 10.8 us  [try_all_shards(): base_arr = jax.lax.all_to_all(piece_next, 'bin', 0, 0)]
    unnamed x7 -> x6, waiting for transfers between devices: 126 us -> 125 us
  transfers between devices with their start and end apart: 7 -> 7, of which waited for: 6 -> 6; matrix products, arithmetic and copies ran while one was open for 24% -> 23% of each run, Pallas kernels for 0% -> 0%
where the time goes in v1:
time: 660 us; the launch traced here: 658 us
  waiting for transfers between devices  373 us (57%)
  local copies, waits for them, and re-layouts  185 us (28%)
  starting transfers between devices  40.1 us (6%)
  blocking collectives  23.7 us (4%)
  between operations  16.6 us (3%)
  matrix products  11.9 us (2%)
  other arithmetic  7.9 us (1%)
    unnamed x6, waiting for transfers between devices  125 us
    all_to_all x1, waiting for transfers between devices, local(): lax.all_to_all(grads.reshape(sources, per_owner, views, emb_dim), DP, spl...  98.8 us
    all_to_all x1, waiting for transfers between devices, local(): lax.all_to_all(outbox.reshape(sources, per_owner, views, emb_dim), DP, sp...  95.6 us
    transpose x1, local copies, waits for them, and re-layouts, local(): jnp.transpose(columns, (0, 3, 2, 1, 4)).reshape(count * views, part_rows)  76.1 us
    reshape x1, local copies, waits for them, and re-layouts, local(): columns = columns.reshape(count * views, *sizes, part_rows // sources)  73.1 us
    all_to_all x1, waiting for transfers between devices, try_all_shards(): base_arr = jax.lax.all_to_all(piece_next, 'bin', 0, 0)  41.9 us
    all_to_all x1, blocking collectives, local(): lax.all_to_all(features.reshape(rows_dev, views, bins_n, part_rows), 'bin...  23.7 us
    all_to_all x1, starting transfers between devices, local(): lax.all_to_all(outbox.reshape(sources, per_owner, views, emb_dim), DP, sp...  19.9 us
  transfers between devices with their start and end apart: 7, of which 6 were waited for; matrix products, arithmetic and copies ran while one was open for 23% of the time, Pallas kernels for 0%

profile of v1, /device:TPU:8, one launch (start us, length us, event | category | flops | bytes accessed | tf_op | source)
XLA Modules:
  0.0 658.2 jit_solution(6494661817010972537)
XLA Ops:
  7.2 3.7 stack.16
  10.9 10.8 %all-to-all-start = ((bf16[4,512,1024]{2,1,0:T(8,128)(2,1)}), bf16[4,512,1024]{2,1,0:T(8,128)(2,1)}, u32[]{:S(2)}, u32[]{:S(2)}) async-start(bf16[4,512,1024]{2,1,0:T(8,128)(2,1)} %stack.16), calls=%async_computation | async-start | bytes 8388608 | tf_op jit(solution)/shard_map/all_to_all | solution.py:77
  22.2 41.9 %all-to-all-done = bf16[4,512,1024]{2,1,0:T(8,128)(2,1)} async-done(((bf16[4,512,1024]{2,1,0:T(8,128)(2,1)}), bf16[4,512,1024]{2,1,0:T(8,128)(2,1)}, u32[]{:S(2)}, u32[]{:S(2)}) %all-to-all-start) | async-done | bytes 4194336 | tf_op jit(solution)/shard_map/all_to_all | solution.py:77
  64.1 3.6 multiply_reduce_fusion
  67.8 0.8 copy-done.4
  69.2 1.1 scatter.12
  70.3 4.3 scatter_fusion
  74.6 1.3 copy-done
  76.0 19.9 %all-to-all-start.1 = ((bf16[128,4,2,1024]{3,2,1,0:T(2,128)(2,1)}), bf16[128,4,2,1024]{3,2,1,0:T(2,128)(2,1)S(1)}, u32[]{:S(2)}, u32[]{:S(2)}) async-start(bf16[128,4,2,1024]{3,2,1,0:T(2,128)(2,1)} %bitcast.63), calls=%async_computation.1 | async-start | bytes 4194304 | tf_op jit(solution)/shard_map/all_to_all | solution.py:96
  99.1 95.6 %all-to-all-done.1 = bf16[128,4,2,1024]{3,2,1,0:T(2,128)(2,1)S(1)} async-done(((bf16[128,4,2,1024]{3,2,1,0:T(2,128)(2,1)}), bf16[128,4,2,1024]{3,2,1,0:T(2,128)(2,1)S(1)}, u32[]{:S(2)}, u32[]{:S(2)}) %all-to-all-start.1) | async-done | bytes 2097184 | tf_op jit(solution)/shard_map/all_to_all | solution.py:96
  195.9 2.7 fusion.31
  200.9 2.7 pad_maximum_fusion
  203.7 9.2 %all-to-all-start.2 = ((bf16[128,4,2,1024]{3,1,2,0:T(4,128)(2,1)}), bf16[128,4,2,1024]{3,1,2,0:T(4,128)(2,1)S(1)}, u32[]{:S(2)}, u32[]{:S(2)}) async-start(bf16[128,4,2,1024]{3,1,2,0:T(4,128)(2,1)} %pad_maximum_fusion), calls=%async_computation.2 | async-start | bytes 4194304 | tf_op jit(solution)/shard_map/all_to_all | solution.py:109
  212.9 98.8 %all-to-all-done.2 = bf16[128,4,2,1024]{3,1,2,0:T(4,128)(2,1)S(1)} async-done(((bf16[128,4,2,1024]{3,1,2,0:T(4,128)(2,1)}), bf16[128,4,2,1024]{3,1,2,0:T(4,128)(2,1)S(1)}, u32[]{:S(2)}, u32[]{:S(2)}) %all-to-all-start.2) | async-done | bytes 2097184 | tf_op jit(solution)/shard_map/all_to_all | solution.py:109
  311.7 3.8 copy.37
  315.5 3.3 gather_fusion
  318.8 2.1 fusion.7
  321.7 23.7 %all_to_all.30 = bf16[128,2,4,512]{3,1,0,2:T(2,128)(2,1)S(1)} all-to-all(bf16[128,2,4,512]{3,1,0,2:T(2,128)(2,1)S(1)} %bitcast.65), channel_id=1, replica_groups=mesh['dx'=4,'dz'=16,'dc'=2,'bin'=4] {'bin'}, dimensions={2} | all-to-all | bytes 2097152 | tf_op jit(solution)/shard_map/all_to_all | solution.py:120
  345.4 73.1 %reshape.161 = bf16[1024,4,16,2,4]{4,3,2,1,0:T(2,128)(2,1)} reshape(bf16[4,128,2,1,512]{4,2,1,0,3:T(2,128)(2,1)S(1)} %bitcast.64) | data formatting | bytes 2097152 | tf_op jit(solution)/shard_map/reshape | solution.py:130
  418.5 76.1 %copy.41 = bf16[1024,2,16,4,4]{0,4,3,2,1:T(4,128)(2,1)S(1)} copy(bf16[1024,2,16,4,4]{4,1,2,3,0:T(2,128)(2,1)} %bitcast.60) | data formatting | bytes 2097152 | tf_op jit(solution)/shard_map/transpose | solution.py:131
  494.9 3.7 copy.39
  498.7 2.2 reshape.159
  500.9 4.2 convolution_bitcast_fusion
  505.3 11.2 %reduce-scatter.6.cloned.1.call-done = f32[256,1024]{0,1:T(8,128)} async-done(((f32[512,1024]{0,1:T(8,128)}), f32[256,1024]{0,1:T(8,128)}) %reduce-scatter.6.cloned.1.call-update) | async-done | bytes 1048592 | tf_op jit(solution)/shard_map/reduce_scatter | solution.py:139
  516.5 2.5 copy.45
  519.1 72.2 %reduce-scatter.8.cloned.1.call-done = f32[16,1024]{1,0:T(8,128)} async-done(((f32[256,1024]{1,0:T(8,128)}), f32[16,1024]{1,0:T(8,128)}) %reduce-scatter.8.cloned.1.call-update) | async-done | bytes 65552
  591.3 1.8 copy.46
  593.2 1.3 dynamic-slice.6
  595.1 1.3 copy.42
  596.4 53.2 %all-reduce.4.cloned.1.call-done = f32[16,1024]{0,1:T(8,128)} async-done(((f32[16,1024]{0,1:T(8,128)}), f32[16,1024]{0,1:T(8,128)}) %all-reduce.4.cloned.1.call-update) | async-done | bytes 65552
  649.6 1.2 dynamic-slice_multiply_fusion
  650.9 0.8 copy.43
  (49 shorter events, 7.3 us)
Async XLA Ops:
  10.9 10.8 %copy-start.8 = (s32[128,1]{0,1:T(1,128)S(1)}, s32[128,1]{0,1:T(1,128)}, u32[]{:S(2)}) copy-start(s32[128,1]{0,1:T(1,128)} %param.9) | copy-start | bytes 1540
  10.9 11.0 %copy-start.6 = (s32[192]{0:T(256)S(1)}, s32[192]{0:T(256)}, u32[]{:S(2)}) copy-start(s32[192]{0:T(256)} %param.10) | copy-start | bytes 2308
  10.9 53.2 %copy-start.2 = (bf16[128,2,2048]{2,1,0:T(2,128)(2,1)S(1)}, bf16[128,2,2048]{2,1,0:T(2,128)(2,1)}, u32[]{:S(2)}) copy-start(bf16[128,2,2048]{2,1,0:T(2,128)(2,1)} %param.7) | copy-start | bytes 3145732
  10.9 53.2 %all-to-all-start = ((bf16[4,512,1024]{2,1,0:T(8,128)(2,1)}), bf16[4,512,1024]{2,1,0:T(8,128)(2,1)}, u32[]{:S(2)}, u32[]{:S(2)}) async-start(bf16[4,512,1024]{2,1,0:T(8,128)(2,1)} %stack.16), calls=%async_computation | async-start | bytes 8388608 | tf_op jit(solution)/shard_map/all_to_all | solution.py:77
  67.7 1.0 copy-start.4
  67.7 1.5 copy-start.7
  74.6 1.4 copy-start
  76.0 22.5 %copy-start.9 = (s32[192]{0:T(256)S(1)}, s32[192]{0:T(256)}, u32[]{:S(2)}) copy-start(s32[192]{0:T(256)} %param.11) | copy-start | bytes 2308
  76.0 118.8 %all-to-all-start.1 = ((bf16[128,4,2,1024]{3,2,1,0:T(2,128)(2,1)}), bf16[128,4,2,1024]{3,2,1,0:T(2,128)(2,1)S(1)}, u32[]{:S(2)}, u32[]{:S(2)}) async-start(bf16[128,4,2,1024]{3,2,1,0:T(2,128)(2,1)} %bitcast.63), calls=%async_computation.1 | async-start | bytes 4194304 | tf_op jit(solution)/shard_map/all_to_all | solution.py:96
  203.7 108.0 %all-to-all-start.2 = ((bf16[128,4,2,1024]{3,1,2,0:T(4,128)(2,1)}), bf16[128,4,2,1024]{3,1,2,0:T(4,128)(2,1)S(1)}, u32[]{:S(2)}, u32[]{:S(2)}) async-start(bf16[128,4,2,1024]{3,1,2,0:T(4,128)(2,1)} %pad_maximum_fusion), calls=%async_computation.2 | async-start | bytes 4194304 | tf_op jit(solution)/shard_map/all_to_all | solution.py:109
  212.9 282.1 %all-gather.2.cloned.1.call-start = ((), (), s32[]{:S(2)}) async-start(), calls=%async_computation.6 | async-start | bytes 2621440 | tf_op jit(solution)/shard_map/all_gather | solution.py:127
  212.9 105.8 %copy-start.5 = (f32[128,2,1024]{2,0,1:T(8,128)S(1)}, f32[128,2,1024]{2,0,1:T(8,128)}, u32[]{:S(2)}) copy-start(f32[128,2,1024]{2,0,1:T(8,128)} %copy-done.4) | copy-start | bytes 3145732
  315.5 5.5 copy-start.3
  320.9 195.6 %reduce-scatter.6.cloned.1.call-start = ((), (), s32[]{:S(2)}) async-start(), calls=%async_computation.7 | async-start | bytes 3145728 | tf_op jit(solution)/shard_map/reduce_scatter | solution.py:139
  505.2 89.9 %copy-start.1 = (bf16[128,2,1024]{2,0,1:T(8,128)(2,1)S(1)}, bf16[128,2,1024]{2,0,1:T(8,128)(2,1)}, u32[]{:S(2)}) copy-start(bf16[128,2,1024]{2,0,1:T(8,128)(2,1)} %fusion.7) | copy-start | bytes 1572868
  505.2 86.1 %reduce-scatter.8.cloned.1.call-start = ((), (), s32[]{:S(2)}) async-start(), calls=%async_computation.8 | async-start | bytes 1114112
  519.0 130.6 %all-reduce.4.cloned.1.call-start = ((), (), s32[]{:S(2)}) async-start(), calls=%async_computation.9 | async-start | bytes 1048576
Sparse Core Ops, SparseCore 0:
  321.0 35.0 all-gather.1
  505.3 11.0 reduce-scatter.5
  519.5 71.7 reduce-scatter.7
  593.5 56.1 all-reduce.3
